TPU v7x, 256 devices: a whole 4x4x8 slice. The times are simulated.
256 devices in a mesh: seq: 8 (over z_lo, core), blk: 32 (over y, z_hi, x).
Axes of the slice: x: 4, y: 4, z: 8 (z_hi: 2, z_lo: 4; z = z_hi * 4 + z_lo), core: 2. Of those that a mesh axis runs over, the one named last changes fastest.
Arguments:
- stream: float32 [4096, 3072], P(('seq', 'blk')), may hold values from -39 to 39
- key_keep: int32 [4096], replicated, may hold values 0 or 1
- positions: int32 [4096, 3], replicated, may hold values from 0 to 63
- lengths: int32 [4], replicated, may hold values from 1 to 2048, 4096 in all
- step_index: int32 [4], replicated, may hold values from 0 to 27
- mod_table: bfloat16 [4, 28, 3, 3072], replicated, may hold values from -4 to 4
- w_qkv: bfloat16 [3072, 9216], P(None, 'blk'), may hold values from -0.109375 to 0.109375
- w_mlp_in: bfloat16 [3072, 12288], P(None, 'blk'), may hold values from -0.109375 to 0.109375
- q_gain: float32 [128], replicated, may hold values from 0.5 to 10
- k_gain: float32 [128], replicated, may hold values from 0.5 to 10
- w_attn_out: bfloat16 [3072, 3072], P('blk'), may hold values from -0.109375 to 0.109375
- w_mlp_out: bfloat16 [12288, 3072], P('blk'), may hold values from -0.0546875 to 0.0546875
Outputs:
- stream_next: float32 [4096, 3072], P(('seq', 'blk'))
Inputs may be any that keep to these rules, and one draw needn't show every extreme that they name: The lengths sum to 4096; the longest request has exactly 2048 tokens.
All inputs are finite; a program needn't handle non-finite values.
Results may differ from a plain program's by a relative error of at most 0.0082.
The roundings to bfloat16 on the way count: a program that leaves them out, or rounds other values in their place, can miss the bound.
Values may be sent and summed in bfloat16 or wider, within the bound.
No kernel may reach another device: no remote copies, remote signals or barrier semaphores. Data moves between devices by JAX's collectives and lax.ppermute only.
A program may use at most 64 MiB of HBM per device.

v0:
```python
import math
import jax
import jax.numpy as jnp
from jax import lax
from jax.sharding import PartitionSpec as P


def rope_table(head_size):
    first_count = head_size // 16
    second = 7 * head_size // 32
    pair_ids = jnp.arange(head_size // 2, dtype=jnp.int32)
    pair_axis = jnp.where(
        pair_ids < first_count, 0, jnp.where(pair_ids < first_count + second, 1, 2)
    )
    pair_local = jnp.where(
        pair_ids < first_count,
        pair_ids,
        jnp.where(
            pair_ids < first_count + second, pair_ids - first_count, pair_ids - first_count - second
        ),
    )
    axis_dims = jnp.where(pair_axis == 0, 2 * first_count, 2 * second)
    frequency = jnp.power(
        jnp.float32(10000.0), -(2 * pair_local).astype(jnp.float32) / axis_dims.astype(jnp.float32)
    )
    return jnp.where(
        jnp.arange(3)[:, None] == pair_axis[None, :], frequency[None, :], jnp.float32(0.0)
    )


def angles_of(places, freq_table):
    return jnp.sum(places.astype(jnp.float32)[:, :, None] * freq_table[None, :, :], axis=1)


def rotate(values, angles):
    paired = values.reshape(values.shape[:-1] + (values.shape[-1] // 2, 2))
    even_part = paired[..., 0]
    odd_part = paired[..., 1]
    cos_part = jnp.cos(angles)[:, None, :]
    sin_part = jnp.sin(angles)[:, None, :]
    turned = jnp.stack(
        [cos_part * even_part - sin_part * odd_part, sin_part * even_part + cos_part * odd_part],
        axis=-1,
    )
    return turned.reshape(values.shape)


def rms_scale(values, gain_vec):
    return values * lax.rsqrt(jnp.mean(values * values, axis=-1, keepdims=True) + 1e-06) * gain_vec


def segment_of(row_ids, request_ends):
    return jnp.sum((row_ids[:, None] >= request_ends[None, :]).astype(jnp.int32), axis=1)


def spread_rows(row_ids, query_rows, block_rows, tok_seq):
    owner = row_ids // query_rows
    within = row_ids % query_rows
    return within // block_rows * tok_seq + owner * block_rows + within % block_rows


def body(
    stream,
    key_keep,
    positions,
    lengths,
    step_index,
    mod_table,
    w_qkv,
    w_mlp_in,
    q_gain,
    k_gain,
    w_attn_out,
    w_mlp_out,
):
    blk_count = lax.axis_size("blk")
    seq_count = lax.axis_size("seq")
    seq_at = lax.axis_index("seq")
    blk_at = lax.axis_index("blk")
    block_rows = stream.shape[0]
    width = stream.shape[1]
    tok_seq = block_rows * blk_count
    head_size = q_gain.shape[0]
    local_heads = width // head_size // seq_count
    requests = mod_table.shape[0]
    step_total = mod_table.shape[1]
    inv_root = 1.0 / math.sqrt(head_size)
    request_ends = jnp.cumsum(lengths)
    own_rows = seq_at * tok_seq + blk_at * block_rows + jnp.arange(block_rows, dtype=jnp.int32)
    own_request = segment_of(own_rows, request_ends)
    step_pick = (jnp.arange(step_total, dtype=jnp.int32)[None, :] == step_index[:, None]).astype(
        jnp.bfloat16
    )
    modulation = jnp.einsum(
        "rs,rsk->rk",
        step_pick,
        mod_table.reshape(requests, step_total, 3 * width),
        preferred_element_type=jnp.float32,
    )
    member = (own_request[:, None] == jnp.arange(requests, dtype=jnp.int32)[None, :]).astype(
        jnp.float32
    )
    token_mod = jnp.dot(member, modulation, precision=lax.Precision.HIGHEST)
    mod_shift = token_mod[:, :width]
    mod_scale = token_mod[:, width : 2 * width]
    mod_gate = token_mod[:, 2 * width :]
    row_mean = jnp.mean(stream, axis=1, keepdims=True)
    centered = stream - row_mean
    row_var = jnp.mean(centered * centered, axis=1, keepdims=True)
    normed = centered * lax.rsqrt(row_var + 1e-06)
    modin = ((1.0 + mod_scale) * normed + mod_shift).astype(jnp.bfloat16)
    qkv_width = w_qkv.shape[1]
    shard_rows = lax.all_gather(modin, "blk", axis=0, tiled=True)
    qkv_part = jnp.dot(shard_rows, w_qkv, preferred_element_type=jnp.float32).astype(jnp.bfloat16)
    mlp_part = jax.nn.gelu(
        jnp.dot(shard_rows, w_mlp_in, preferred_element_type=jnp.float32), approximate=True
    ).astype(jnp.bfloat16)
    joined = jnp.concatenate([qkv_part, mlp_part], axis=1)
    qkv_cols = joined[:, :qkv_width]
    mlp_act = joined[:, qkv_width:]
    heads_in = lax.all_to_all(
        lax.all_to_all(qkv_cols, "blk", split_axis=0, concat_axis=1, tiled=True),
        "seq",
        split_axis=1,
        concat_axis=0,
        tiled=True,
    )
    query_rows = heads_in.shape[0]
    heads4 = heads_in.reshape(query_rows, local_heads, 3, head_size)
    query_ids = spread_rows(
        blk_at * query_rows + jnp.arange(query_rows, dtype=jnp.int32),
        query_rows,
        block_rows,
        tok_seq,
    )
    query_request = segment_of(query_ids, request_ends)
    angles = angles_of(jnp.take(positions, query_ids, axis=0), rope_table(head_size))
    query_rot = rotate(rms_scale(heads4[:, :, 0].astype(jnp.float32), q_gain), angles).astype(
        jnp.bfloat16
    )
    key_rot = rotate(rms_scale(heads4[:, :, 1].astype(jnp.float32), k_gain), angles).astype(
        jnp.bfloat16
    )
    value_rows = heads4[:, :, 2]
    run_top = jnp.full((query_rows, local_heads), -1e30, jnp.float32)
    key_part = lax.all_gather(key_rot, "blk", axis=0, tiled=True)
    value_part = lax.all_gather(value_rows, "blk", axis=0, tiled=True)
    key_ids = spread_rows(
        jnp.arange(key_part.shape[0], dtype=jnp.int32), query_rows, block_rows, tok_seq
    )
    key_request = segment_of(key_ids, request_ends)
    kept = jnp.take(key_keep, key_ids) == 1
    visible = (
        (query_request[:, None] == key_request[None, :])
        & (kept[None, :] | (query_ids[:, None] == key_ids[None, :]))
    )[:, None, :]
    scores = (
        jnp.einsum("qhd,khd->qhk", query_rot, key_part, preferred_element_type=jnp.float32)
        * inv_root
    )
    row_high = jnp.max(jnp.where(visible, scores, -1e30), axis=2)
    new_top = jnp.maximum(run_top, row_high)
    weights = jnp.where(visible, jnp.exp(scores - new_top[:, :, None]), 0.0)
    run_norm = jnp.sum(weights, axis=2)
    run_sum = jnp.einsum(
        "qhk,khd->qhd", weights.astype(jnp.bfloat16), value_part, preferred_element_type=jnp.float32
    )
    run_top, run_norm, run_sum = (new_top, run_norm, run_sum)
    attended = (run_sum / run_norm[:, :, None]).astype(jnp.bfloat16)
    attended = attended.reshape(query_rows, local_heads * head_size)
    attn_local = lax.all_to_all(
        lax.all_to_all(attended, "seq", split_axis=0, concat_axis=1, tiled=True),
        "blk",
        split_axis=1,
        concat_axis=0,
        tiled=True,
    )
    mlp_part = mlp_act
    summed = lax.psum_scatter(
        (
            jnp.dot(attn_local, w_attn_out, preferred_element_type=jnp.float32)
            + jnp.dot(mlp_part, w_mlp_out, preferred_element_type=jnp.float32)
        ).astype(jnp.bfloat16),
        "blk",
        scatter_dimension=0,
        tiled=True,
    ).astype(jnp.float32)
    return stream + mod_gate * summed


def solution(mesh):
    in_specs = (
        P(("seq", "blk"), None),
        P(),
        P(),
        P(),
        P(),
        P(),
        P(None, "blk"),
        P(None, "blk"),
        P(),
        P(),
        P("blk", None),
        P("blk", None),
    )
    out_specs = P(("seq", "blk"), None)
    return jax.shard_map(body, mesh=mesh, in_specs=in_specs, out_specs=out_specs, check_vma=False)
```

profile of v0, /device:TPU:2, one launch (start us, length us, event | category | flops | bytes accessed | tf_op | source)
XLA Modules:
  0.0 693.5 jit_solution(4572374142016408520)
XLA Ops:
  10.6 2.8 fusion.11
  14.7 102.6 %all-gather.5.cloned.1.call-done = bf16[512,3072]{1,0:T(8,128)(2,1)} async-done(((bf16[16,3072]{1,0:T(8,128)(2,1)}), bf16[512,3072]{1,0:T(8,128)(2,1)}) %all-gather.5.cloned.1.call-update) | async-done | bytes 3145744 | tf_op jit(solution)/shard_map/all_gather | solution.py:113
  117.3 3.5 convolution_convert_fusion
  121.8 6.2 all-to-all-start
  129.5 2.8 copy.83
  132.3 2.8 gather_fusion.1
  136.7 5.6 all-to-all-done
  145.3 3.9 all-to-all-start.1
  150.8 8.9 %all-to-all-done.1 = bf16[16,8,1152]{2,0,1:T(8,128)(2,1)S(1)} async-done(((bf16[16,8,1152]{2,0,1:T(8,128)(2,1)}), bf16[16,8,1152]{2,0,1:T(8,128)(2,1)S(1)}, u32[]{:S(2)}, u32[]{:S(2)}) %all-to-all-start.1) | async-done | bytes 294944 | tf_op jit(solution)/shard_map/all_to_all | solution.py:121
  164.5 1.7 copy.86
  170.5 2.0 subtract_convert_fusion
  174.7 23.0 %gather_fusion = s32[4096]{0:T(1024)S(1)} fusion(s32[4096]{0:T(1024)S(1)} %copy-done.1, s32[4096]{0:T(1024)S(1)} %broadcast_clamp_fusion), kind=kCustom, calls=%fused_computation | custom fusion | bytes 49152 | tf_op jit(solution)/shard_map/jit(_take)/gather | solution.py:152
  198.0 4.5 or_and_fusion
  202.8 66.0 %all-gather.7.cloned.1.call-done = bf16[4096,3,128]{2,0,1:T(8,128)(2,1)} async-done(((bf16[128,3,128]{2,0,1:T(8,128)(2,1)}), bf16[4096,3,128]{2,0,1:T(8,128)(2,1)}) %all-gather.7.cloned.1.call-update) | async-done | bytes 3145744 | tf_op jit(solution)/shard_map/all_gather | solution.py:146
  268.8 3.2 fusion
  272.1 2.6 copy-done.2
  275.9 106.2 %all-gather.9.cloned.1.call-done = bf16[4096,3,1,128]{0,3,1,2:T(8,128)(2,1)} async-done(((bf16[128,3,1,128]{0,3,1,2:T(8,128)(2,1)}), bf16[4096,3,1,128]{0,3,1,2:T(8,128)(2,1)}) %all-gather.9.cloned.1.call-update) | async-done | bytes 3145744 | tf_op jit(solution)/shard_map/all_gather | solution.py:147
  382.1 5.3 fusion.23
  387.7 8.7 %all_to_all.67 = bf16[8,16,384]{2,1,0:T(8,128)(2,1)S(1)} all-to-all(bf16[8,16,384]{2,1,0:T(8,128)(2,1)S(1)} %all_to_all.56), channel_id=1, replica_groups=mesh['seq'=8,'blk'=32] {'seq'}, dimensions={0} | all-to-all | bytes 196608 | tf_op jit(solution)/shard_map/all_to_all | solution.py:172
  396.6 19.6 %all_to_all.68 = bf16[16,32,96]{2,0,1:T(8,128)(2,1)S(1)} all-to-all(bf16[16,32,96]{2,0,1:T(8,128)(2,1)S(1)} %copy.98), channel_id=1, replica_groups=mesh['seq'=8,'blk'=32] {'blk'}, dimensions={1} | all-to-all | bytes 196608 | tf_op jit(solution)/shard_map/all_to_all | solution.py:171
  416.2 4.7 fusion.90
  420.9 9.6 %add_convert_fusion = bf16[512,3072]{1,0:T(8,128)(2,1)} fusion(f32[512,3072]{1,0:T(8,128)} %fusion.90, bf16[384,3072]{1,0:T(8,128)(2,1)S(1)} %copy-done, bf16[512,3072]{1,0:T(8,128)(2,1)} %all-gather.5.cloned.1.call-done, bf16[3072,384]{1,0:T(8,128)(2,1)} %param.19), kind=kOutput, calls=%fused_computation.7 | convolution fusion | flops 2420834304 | bytes 17301504 | tf_op jit(solution)/shard_map/dot_general | solution.py:182
  430.5 254.9 %reduce-scatter.2.cloned.1.call-done = bf16[16,3072]{1,0:T(8,128)(2,1)} async-done(((bf16[512,3072]{1,0:T(8,128)(2,1)}), bf16[16,3072]{1,0:T(8,128)(2,1)}) %reduce-scatter.2.cloned.1.call-update) | async-done | bytes 98320 | tf_op jit(solution)/shard_map/reduce_scatter | solution.py:179
  685.4 1.6 fusion.43
  (86 shorter events, 27.1 us)
Async XLA Ops:
  6.5 414.4 %copy-start = (bf16[384,3072]{1,0:T(8,128)(2,1)S(1)}, bf16[384,3072]{1,0:T(8,128)(2,1)}, u32[]{:S(2)}) copy-start(bf16[384,3072]{1,0:T(8,128)(2,1)} %param.23) | copy-start | bytes 7077892
  6.5 7.3 %copy-start.3 = (f32[16,3072]{1,0:T(8,128)S(1)}, f32[16,3072]{1,0:T(8,128)}, u32[]{:S(2)}) copy-start(f32[16,3072]{1,0:T(8,128)} %param.12) | copy-start | bytes 589828
  6.5 110.8 %all-gather.5.cloned.1.call-start = ((), (), s32[]{:S(2)}) async-start(), calls=%async_computation.5 | async-start | bytes 3244032 | tf_op jit(solution)/shard_map/all_gather | solution.py:113
  10.5 4.2 copy-start.11
  14.7 113.3 %copy-start.9 = (f32[128]{0:T(128)S(1)}, f32[128]{0:T(128)}, u32[]{:S(2)}) copy-start(f32[128]{0:T(128)} %param.21) | copy-start | bytes 1540
  14.7 114.1 %copy-start.10 = (f32[128]{0:T(128)S(1)}, f32[128]{0:T(128)}, u32[]{:S(2)}) copy-start(f32[128]{0:T(128)} %param.20) | copy-start | bytes 1540
  121.8 20.5 %all-to-all-start = ((bf16[32,16,288]{2,1,0:T(8,128)(2,1)}), bf16[32,16,288]{2,1,0:T(8,128)(2,1)S(1)}, u32[]{:S(2)}, u32[]{:S(2)}) async-start(bf16[32,16,288]{2,1,0:T(8,128)(2,1)} %bitcast.68), calls=%async_computation | async-start | bytes 786432 | tf_op jit(solution)/shard_map/all_to_all | solution.py:122
  145.3 14.3 %all-to-all-start.1 = ((bf16[16,8,1152]{2,0,1:T(8,128)(2,1)}), bf16[16,8,1152]{2,0,1:T(8,128)(2,1)S(1)}, u32[]{:S(2)}, u32[]{:S(2)}) async-start(bf16[16,8,1152]{2,0,1:T(8,128)(2,1)} %copy.81), calls=%async_computation.1 | async-start | bytes 589824 | tf_op jit(solution)/shard_map/all_to_all | solution.py:121
  149.2 119.6 %all-gather.7.cloned.1.call-start = ((), (), s32[]{:S(2)}) async-start(), calls=%async_computation.6 | async-start | bytes 3244032 | tf_op jit(solution)/shard_map/all_gather | solution.py:146
  159.6 0.7 copy-start.5
  160.3 14.3 %copy-start.1 = (s32[4096]{0:T(1024)S(1)}, s32[4096]{0:T(1024)}, u32[]{:S(2)}) copy-start(s32[4096]{0:T(1024)} %param.13) | copy-start | bytes 49156
  162.5 11.0 %copy-start.6 = (bf16[128,3,1,128]{3,2,1,0:T(2,128)(2,1)S(1)}, bf16[128,3,1,128]{3,2,1,0:T(2,128)(2,1)}, u32[]{:S(2)}) copy-start(bf16[128,3,1,128]{3,2,1,0:T(2,128)(2,1)} %get-tuple-element.5) | copy-start | bytes 294916
  173.5 208.7 %all-gather.9.cloned.1.call-start = ((), (), s32[]{:S(2)}) async-start(), calls=%async_computation.8 | async-start | bytes 3244032 | tf_op jit(solution)/shard_map/all_gather | solution.py:147
  174.3 511.1 %reduce-scatter.2.cloned.1.call-start = ((), (), s32[]{:S(2)}) async-start(), calls=%async_computation.7 | async-start | bytes 3244032 | tf_op jit(solution)/shard_map/reduce_scatter | solution.py:179
  174.7 23.1 %copy-start.12 = (s32[4,1]{0,1:T(1,128)S(1)}, s32[4,1]{0,1:T(1,128)}, u32[]{:S(2)}) copy-start(s32[4,1]{0,1:T(1,128)} %copy-done.11) | copy-start | bytes 52
  174.7 27.9 %copy-start.7 = (bf16[128,3,64,1]{0,3,2,1:T(2,128)(2,1)S(1)}, bf16[128,3,64,1]{0,3,2,1:T(2,128)(2,1)}, u32[]{:S(2)}) copy-start(bf16[128,3,64,1]{0,3,2,1:T(2,128)(2,1)} %get-tuple-element.8) | copy-start | bytes 147460
  174.7 27.9 %copy-start.8 = (bf16[128,3,64,1]{0,3,2,1:T(2,128)(2,1)S(1)}, bf16[128,3,64,1]{0,3,2,1:T(2,128)(2,1)}, u32[]{:S(2)}) copy-start(bf16[128,3,64,1]{0,3,2,1:T(2,128)(2,1)} %get-tuple-element.9) | copy-start | bytes 147460
  268.8 5.9 copy-start.4
  272.0 2.7 copy-start.2
Sparse Core Ops, SparseCore 0:
  14.8 102.5 all-gather.4
  173.6 95.2 all-gather.6
  272.0 110.0 all-gather.8
  430.6 254.7 reduce-scatter.1
where the time goes:
time: 694 us
  waiting for transfers between devices  544 us (78%)
  local copies, waits for them, and re-layouts  45.8 us (7%)
  matrix products  29.6 us (4%)
  blocking collectives  28.3 us (4%)
  other arithmetic  21.7 us (3%)
  between operations  13.4 us (2%)
  starting transfers between devices  10.4 us (1%)
    reduce_scatter x1, waiting for transfers between devices, body(): lax.psum_scatter((jnp.dot(attn_local, w_attn_out, preferred_element_type=...  255 us
    all_gather x1, waiting for transfers between devices, body(): value_part = lax.all_gather(value_rows, 'blk', axis=0, tiled=True)  106 us
    all_gather x1, waiting for transfers between devices, body(): shard_rows = lax.all_gather(modin, 'blk', axis=0, tiled=True)  103 us
    all_gather x1, waiting for transfers between devices, body(): key_part = lax.all_gather(key_rot, 'blk', axis=0, tiled=True)  66 us
    gather x1, local copies, waits for them, and re-layouts, body(): kept = jnp.take(key_keep, key_ids) == 1  23 us
    all_to_all x1, blocking collectives, body(): lax.all_to_all(lax.all_to_all(attended, 'seq', split_axis=0, concat_axis=...  19.6 us
  transfers between devices with their start and end apart: 6, of which 6 were waited for; matrix products, arithmetic and copies ran while one was open for 6% of the time, Pallas kernels for 0%

commit v1 on v0

--- a/solution.py
+++ b/solution.py
@@ -143,7 +143,9 @@
     )
     value_rows = heads4[:, :, 2]
     run_top = jnp.full((query_rows, local_heads), -1e30, jnp.float32)
-    key_part = lax.all_gather(key_rot, "blk", axis=0, tiled=True)
+    key_part = jnp.concatenate(
+        lax.all_to_all(jnp.stack([key_rot] * lax.axis_size("blk")), "blk", 0, 0), axis=0
+    )
     value_part = lax.all_gather(value_rows, "blk", axis=0, tiled=True)
     key_ids = spread_rows(
         jnp.arange(key_part.shape[0], dtype=jnp.int32), query_rows, block_rows, tok_seq

time: 694 us -> 638 us (0.919)
  waiting for transfers between devices: 544 us -> 483 us
    all_gather x1 -> x0, waiting for transfers between devices: 66 us -> none  [body(): key_part = lax.all_gather(key_rot, 'blk', axis=0, tiled=True)]
    all_to_all x0 -> x1, waiting for transfers between devices: none -> 49.1 us  [body(): lax.all_to_all(jnp.stack([key_rot] * lax.axis_size('blk')), 'blk', 0, 0)]
    all_gather x1, waiting for transfers between devices: 106 us -> 61.4 us  [body(): value_part = lax.all_gather(value_rows, 'blk', axis=0, tiled=True)]
  transfers between devices with their start and end apart: 6 -> 6, of which waited for: 6 -> 6; matrix products, arithmetic and copies ran while one was open for 6% -> 7% of each run, Pallas kernels for 0% -> 0%
where the time goes in v1:
time: 638 us; the launch traced here: 637 us
  waiting for transfers between devices  483 us (76%)
  local copies, waits for them, and re-layouts  49.3 us (8%)
  blocking collectives  28.3 us (4%)
  matrix products  27.6 us (4%)
  other arithmetic  19.1 us (3%)
  starting transfers between devices  16.8 us (3%)
  between operations  13.4 us (2%)
    reduce_scatter x1, waiting for transfers between devices, body(): lax.psum_scatter((jnp.dot(attn_local, w_attn_out, preferred_element_type=...  255 us
    all_gather x1, waiting for transfers between devices, body(): shard_rows = lax.all_gather(modin, 'blk', axis=0, tiled=True)  103 us
    all_gather x1, waiting for transfers between devices, body(): value_part = lax.all_gather(value_rows, 'blk', axis=0, tiled=True)  61.4 us
    all_to_all x1, waiting for transfers between devices, body(): lax.all_to_all(jnp.stack([key_rot] * lax.axis_size('blk')), 'blk', 0, 0)  49.1 us
    gather x1, local copies, waits for them, and re-layouts, body(): kept = jnp.take(key_keep, key_ids) == 1  23 us
    all_to_all x1, blocking collectives, body(): lax.all_to_all(lax.all_to_all(attended, 'seq', split_axis=0, concat_axis=...  19.6 us
  transfers between devices with their start and end apart: 6, of which 6 were waited for; matrix products, arithmetic and copies ran while one was open for 7% of the time, Pallas kernels for 0%

profile of v1, /device:TPU:2, one launch (start us, length us, event | category | flops | bytes accessed | tf_op | source)
XLA Modules:
  0.0 637.2 jit_solution(6468055761476219795)
XLA Ops:
  10.6 2.8 fusion.11
  14.7 102.6 %all-gather.4.cloned.1.call-done = bf16[512,3072]{1,0:T(8,128)(2,1)} async-done(((bf16[16,3072]{1,0:T(8,128)(2,1)}), bf16[512,3072]{1,0:T(8,128)(2,1)}) %all-gather.4.cloned.1.call-update) | async-done | bytes 3145744 | tf_op jit(solution)/shard_map/all_gather | solution.py:113
  117.3 3.5 convolution_convert_fusion
  121.8 6.2 all-to-all-start
  129.5 2.8 copy.85
  132.3 2.8 gather_fusion.1
  136.7 5.6 all-to-all-done
  145.3 3.9 all-to-all-start.1
  150.7 8.9 %all-to-all-done.1 = bf16[16,8,1152]{2,0,1:T(8,128)(2,1)S(1)} async-done(((bf16[16,8,1152]{2,0,1:T(8,128)(2,1)}), bf16[16,8,1152]{2,0,1:T(8,128)(2,1)S(1)}, u32[]{:S(2)}, u32[]{:S(2)}) %all-to-all-start.1) | async-done | bytes 294944 | tf_op jit(solution)/shard_map/all_to_all | solution.py:121
  167.2 2.0 subtract_convert_fusion
  169.5 2.5 stack.9
  172.0 6.5 %all-to-all-start.2 = ((bf16[32,128,3,128]{3,1,2,0:T(8,128)(2,1)}), bf16[32,128,3,128]{3,1,2,0:T(8,128)(2,1)}, u32[]{:S(2)}, u32[]{:S(2)}) async-start(bf16[32,128,3,128]{3,1,2,0:T(8,128)(2,1)} %stack.9), calls=%async_computation.2 | async-start | bytes 6291456 | tf_op jit(solution)/shard_map/all_to_all | solution.py:147
  179.8 23.0 %gather_fusion = s32[4096]{0:T(1024)S(1)} fusion(s32[4096]{0:T(1024)S(1)} %copy-done.1, s32[4096]{0:T(1024)S(1)} %broadcast_clamp_fusion), kind=kCustom, calls=%fused_computation | custom fusion | bytes 49152 | tf_op jit(solution)/shard_map/jit(_take)/gather | solution.py:154
  203.1 4.5 or_and_fusion
  207.9 49.1 %all-to-all-done.2 = bf16[32,128,3,128]{3,1,2,0:T(8,128)(2,1)} async-done(((bf16[32,128,3,128]{3,1,2,0:T(8,128)(2,1)}), bf16[32,128,3,128]{3,1,2,0:T(8,128)(2,1)}, u32[]{:S(2)}, u32[]{:S(2)}) %all-to-all-start.2) | async-done | bytes 3145760 | tf_op jit(solution)/shard_map/all_to_all | solution.py:147
  257.0 2.3 copy.92
  260.6 2.6 copy-done.2
  264.4 61.4 %all-gather.6.cloned.1.call-done = bf16[4096,3,1,128]{0,3,1,2:T(8,128)(2,1)} async-done(((bf16[128,3,1,128]{0,3,1,2:T(8,128)(2,1)}), bf16[4096,3,1,128]{0,3,1,2:T(8,128)(2,1)}) %all-gather.6.cloned.1.call-update) | async-done | bytes 3145744 | tf_op jit(solution)/shard_map/all_gather | solution.py:149
  325.8 5.3 fusion.23
  331.3 8.7 %all_to_all.72 = bf16[8,16,384]{2,1,0:T(8,128)(2,1)S(1)} all-to-all(bf16[8,16,384]{2,1,0:T(8,128)(2,1)S(1)} %all_to_all.60), channel_id=1, replica_groups=mesh['seq'=8,'blk'=32] {'seq'}, dimensions={0} | all-to-all | bytes 196608 | tf_op jit(solution)/shard_map/all_to_all | solution.py:174
  340.2 19.6 %all_to_all.73 = bf16[16,32,96]{2,0,1:T(8,128)(2,1)S(1)} all-to-all(bf16[16,32,96]{2,0,1:T(8,128)(2,1)S(1)} %copy.101), channel_id=1, replica_groups=mesh['seq'=8,'blk'=32] {'blk'}, dimensions={1} | all-to-all | bytes 196608 | tf_op jit(solution)/shard_map/all_to_all | solution.py:173
  359.9 4.7 fusion.90
  364.5 9.6 %add_convert_fusion = bf16[512,3072]{1,0:T(8,128)(2,1)} fusion(f32[512,3072]{1,0:T(8,128)} %fusion.90, bf16[384,3072]{1,0:T(8,128)(2,1)S(1)} %copy-done, bf16[512,3072]{1,0:T(8,128)(2,1)} %all-gather.4.cloned.1.call-done, bf16[3072,384]{1,0:T(8,128)(2,1)} %param.19), kind=kOutput, calls=%fused_computation.7 | convolution fusion | flops 2420834304 | bytes 17301504 | tf_op jit(solution)/shard_map/dot_general | solution.py:184
  374.2 254.9 %reduce-scatter.2.cloned.1.call-done = bf16[16,3072]{1,0:T(8,128)(2,1)} async-done(((bf16[512,3072]{1,0:T(8,128)(2,1)}), bf16[16,3072]{1,0:T(8,128)(2,1)}) %reduce-scatter.2.cloned.1.call-update) | async-done | bytes 98320 | tf_op jit(solution)/shard_map/reduce_scatter | solution.py:181
  (87 shorter events, 27.6 us)
Async XLA Ops:
  6.5 358.0 %copy-start = (bf16[384,3072]{1,0:T(8,128)(2,1)S(1)}, bf16[384,3072]{1,0:T(8,128)(2,1)}, u32[]{:S(2)}) copy-start(bf16[384,3072]{1,0:T(8,128)(2,1)} %param.23) | copy-start | bytes 7077892
  6.5 7.3 %copy-start.3 = (f32[16,3072]{1,0:T(8,128)S(1)}, f32[16,3072]{1,0:T(8,128)}, u32[]{:S(2)}) copy-start(f32[16,3072]{1,0:T(8,128)} %param.12) | copy-start | bytes 589828
  6.5 110.8 %all-gather.4.cloned.1.call-start = ((), (), s32[]{:S(2)}) async-start(), calls=%async_computation.6 | async-start | bytes 3244032 | tf_op jit(solution)/shard_map/all_gather | solution.py:113
  10.5 4.1 copy-start.11
  14.7 113.3 %copy-start.9 = (f32[128]{0:T(128)S(1)}, f32[128]{0:T(128)}, u32[]{:S(2)}) copy-start(f32[128]{0:T(128)} %param.21) | copy-start | bytes 1540
  14.7 114.1 %copy-start.10 = (f32[128]{0:T(128)S(1)}, f32[128]{0:T(128)}, u32[]{:S(2)}) copy-start(f32[128]{0:T(128)} %param.20) | copy-start | bytes 1540
  121.8 20.5 %all-to-all-start = ((bf16[32,16,288]{2,1,0:T(8,128)(2,1)}), bf16[32,16,288]{2,1,0:T(8,128)(2,1)S(1)}, u32[]{:S(2)}, u32[]{:S(2)}) async-start(bf16[32,16,288]{2,1,0:T(8,128)(2,1)} %bitcast.70), calls=%async_computation | async-start | bytes 786432 | tf_op jit(solution)/shard_map/all_to_all | solution.py:122
  145.3 14.3 %all-to-all-start.1 = ((bf16[16,8,1152]{2,0,1:T(8,128)(2,1)}), bf16[16,8,1152]{2,0,1:T(8,128)(2,1)S(1)}, u32[]{:S(2)}, u32[]{:S(2)}) async-start(bf16[16,8,1152]{2,0,1:T(8,128)(2,1)} %copy.83), calls=%async_computation.1 | async-start | bytes 589824 | tf_op jit(solution)/shard_map/all_to_all | solution.py:121
  159.6 0.7 copy-start.5
  172.0 6.6 %copy-start.6 = (bf16[128,3,1,128]{3,2,1,0:T(2,128)(2,1)S(1)}, bf16[128,3,1,128]{3,2,1,0:T(2,128)(2,1)}, u32[]{:S(2)}) copy-start(bf16[128,3,1,128]{3,2,1,0:T(2,128)(2,1)} %get-tuple-element.5) | copy-start | bytes 294916
  172.0 7.7 %copy-start.1 = (s32[4096]{0:T(1024)S(1)}, s32[4096]{0:T(1024)}, u32[]{:S(2)}) copy-start(s32[4096]{0:T(1024)} %param.13) | copy-start | bytes 49156
  172.0 85.0 %all-to-all-start.2 = ((bf16[32,128,3,128]{3,1,2,0:T(8,128)(2,1)}), bf16[32,128,3,128]{3,1,2,0:T(8,128)(2,1)}, u32[]{:S(2)}, u32[]{:S(2)}) async-start(bf16[32,128,3,128]{3,1,2,0:T(8,128)(2,1)} %stack.9), calls=%async_computation.2 | async-start | bytes 6291456 | tf_op jit(solution)/shard_map/all_to_all | solution.py:147
  178.5 147.2 %all-gather.6.cloned.1.call-start = ((), (), s32[]{:S(2)}) async-start(), calls=%async_computation.8 | async-start | bytes 3244032 | tf_op jit(solution)/shard_map/all_gather | solution.py:149
  179.4 449.7 %reduce-scatter.2.cloned.1.call-start = ((), (), s32[]{:S(2)}) async-start(), calls=%async_computation.7 | async-start | bytes 3244032 | tf_op jit(solution)/shard_map/reduce_scatter | solution.py:181
  179.7 23.1 %copy-start.12 = (s32[4,1]{0,1:T(1,128)S(1)}, s32[4,1]{0,1:T(1,128)}, u32[]{:S(2)}) copy-start(s32[4,1]{0,1:T(1,128)} %copy-done.11) | copy-start | bytes 52
  179.7 27.9 %copy-start.7 = (bf16[128,3,64,1]{0,3,2,1:T(2,128)(2,1)S(1)}, bf16[128,3,64,1]{0,3,2,1:T(2,128)(2,1)}, u32[]{:S(2)}) copy-start(bf16[128,3,64,1]{0,3,2,1:T(2,128)(2,1)} %get-tuple-element.8) | copy-start | bytes 147460
  179.7 27.9 %copy-start.8 = (bf16[128,3,64,1]{0,3,2,1:T(2,128)(2,1)S(1)}, bf16[128,3,64,1]{0,3,2,1:T(2,128)(2,1)}, u32[]{:S(2)}) copy-start(bf16[128,3,64,1]{0,3,2,1:T(2,128)(2,1)} %get-tuple-element.9) | copy-start | bytes 147460
  257.0 2.4 copy-start.4
  260.5 2.7 copy-start.2
Sparse Core Ops, SparseCore 0:
  14.8 102.5 all-gather.3
  182.6 143.1 all-gather.5
  374.3 254.7 reduce-scatter.1
